TPU v7x, 512 devices: a whole 4x8x8 slice. The times are simulated.
512 devices in a mesh: req: 64 (over x, y, core), tp: 8 (over z).
Axes of the slice: x: 4, y: 8, z: 8, core: 2. Of those that a mesh axis runs over, the one named last changes fastest.
Arguments:
- vit_context: bfloat16 [32768, 4096], P('req', 'tp'), may hold values from -6 to 6
- vision_residual: bfloat16 [32768, 4096], P('req', 'tp'), may hold values from -75 to 75
- out_weight: bfloat16 [4096, 4096], P('tp', 'req'), may hold values from -0.09375 to 0.09375
- layer_scale: float32 [4096], P('tp'), may hold values from 0.2 to 2
- prompt: bfloat16 [64, 256, 4096], P('req', None, 'tp'), may hold values from -75 to 75
- prompt_len: int32 [64], P('req'), may hold values from 128 to 256
- image_at: int32 [64], P('req'), may hold values from 0 to 128
- grid_sizes: int32 [128, 2], replicated, may hold values from 7 to 8, as said below
- image_owner: int32 [128], replicated, may hold values from 0 to 63, as said below
- norm_gain: float32 [4096], replicated, may hold values from 0.5 to 1.5
- qkv_weight: bfloat16 [4096, 6144], P('req', 'tp'), may hold values from -0.09375 to 0.09375
Outputs:
- qkv: bfloat16 [24576, 6144], P('req', 'tp')
Inputs may be any that keep to these rules, and one draw needn't show every extreme that they name: `image_owner`: each request owns exactly 2 images. `grid_sizes`: each side is 7 or 8; in every draw the images of some request are all 8 by 8, so that request has exactly 128 merged rows.
All inputs are finite; a program needn't handle non-finite values.
Results may differ from a plain program's by a relative error of at most 0.008.
Values may be sent and summed in bfloat16 or wider, within the bound.
No kernel may reach another device: no remote copies, remote signals or barrier semaphores. Data moves between devices by JAX's collectives and lax.ppermute only.
A program may use at most 64 MiB of HBM per device.

v0:
```python
import jax
import jax.numpy as jnp
from jax import lax
from jax.sharding import Mesh, PartitionSpec as P

HEAD = 128
GROUP = 4
IMG_MAX = 128
REQ = ("rx", "ry", "rc")


def request_plan(grid_sizes, image_owner, requests):
    image_rows = grid_sizes[:, 0] * grid_sizes[:, 1]
    member = (image_owner[:, None] == jnp.arange(requests, dtype=jnp.int32)[None, :]).astype(
        jnp.int32
    )
    counts = jnp.sum(image_rows[:, None] * member, axis=0)
    starts = jnp.cumsum(counts) - counts
    return (counts, starts)


def rope_tables(count):
    half_size = HEAD // 2
    exponent = jnp.arange(half_size, dtype=jnp.float32) * (2.0 / HEAD)
    frequency = jnp.exp(-exponent * jnp.log(jnp.float32(500000.0)))
    angles = jnp.arange(count, dtype=jnp.float32)[:, None] * frequency[None, :]
    return (jnp.cos(angles), jnp.sin(angles))


def apply_rope(projected, cosine_table, sine_table):
    seq_rows = projected.shape[0]
    head_blocks = projected.reshape(seq_rows, -1, GROUP + 2, HEAD)
    turning = head_blocks[:, :, : GROUP + 1, :]
    first_half = turning[..., : HEAD // 2]
    second_half = turning[..., HEAD // 2 :]
    cosine_wide = cosine_table[:, None, None, :]
    sine_wide = sine_table[:, None, None, :]
    turned = jnp.concatenate(
        [
            first_half * cosine_wide - second_half * sine_wide,
            second_half * cosine_wide + first_half * sine_wide,
        ],
        axis=-1,
    )
    head_blocks = jnp.concatenate([turned, head_blocks[:, :, GROUP + 1 :, :]], axis=2)
    return head_blocks.reshape(seq_rows, -1)


def normalize(embedded, norm_gain):
    values = embedded.astype(jnp.float32)
    mean_square = jnp.mean(values * values, axis=-1, keepdims=True)
    return (values * lax.rsqrt(mean_square + 1e-05) * norm_gain[None, :]).astype(jnp.bfloat16)


def gather_features(rows, tp_count):
    copies = jnp.broadcast_to(rows[None], (tp_count,) + rows.shape)
    blocks = lax.all_to_all(copies, "tp", 0, 0, tiled=True)
    return blocks.transpose(1, 0, 2).reshape(rows.shape[0], -1)


def shift(value, axis, step):
    size = lax.axis_size(axis)
    return lax.ppermute(value, axis, [(k, (k + step) % size) for k in range(size)])


def ring_gather(value, axis):
    size = lax.axis_size(axis)
    return jnp.stack([value] + [shift(value, axis, -step) for step in range(1, size)], axis=0)


def eight_gather(value, axis):
    from_next = shift(value, axis, -1)
    from_last = shift(value, axis, 1)
    three = jnp.stack([from_last, value, from_next], axis=0)
    far_next = shift(three, axis, -3)
    far_last = shift(three, axis, 3)
    return jnp.stack(
        [
            value,
            from_next,
            far_next[0],
            far_next[1],
            far_next[2],
            far_last[1],
            far_last[2],
            from_last,
        ],
        axis=0,
    )


def gather_plane(shard):
    by_y = eight_gather(shard, "ry") if lax.axis_size("ry") == 8 else ring_gather(shard, "ry")
    return ring_gather(by_y, "rx")


def shards(
    vit_context,
    vision_residual,
    out_weight,
    layer_scale,
    prompt,
    prompt_len,
    image_at,
    grid_sizes,
    image_owner,
    norm_gain,
    qkv_weight,
):
    requests = lax.axis_size(REQ)
    device_index = lax.axis_index(REQ)
    feature_width = vit_context.shape[1]
    merged_context = jnp.mean(
        vit_context.astype(jnp.float32).reshape(-1, 4, feature_width), axis=1
    ).astype(jnp.bfloat16)
    merged_residual = jnp.mean(
        vision_residual.astype(jnp.float32).reshape(-1, 4, feature_width), axis=1
    )
    swap = [(0, 1), (1, 0)]
    core = lax.axis_index("rc")
    context_pair = jnp.stack([merged_context, lax.ppermute(merged_context, "rc", swap)])
    context_ring = ring_gather(context_pair, "rx")
    weight_ring = (
        eight_gather(out_weight, "ry")
        if lax.axis_size("ry") == 8
        else ring_gather(out_weight, "ry")
    )
    parts = jnp.einsum(
        "dcgk,ykn->dcgyn", context_ring, weight_ring, preferred_element_type=jnp.float32
    ).astype(jnp.bfloat16)
    from_partner = lax.ppermute(parts[:, 1], "rc", swap)
    both = jnp.stack([parts[:, 0], from_partner], axis=-2)
    x_count = lax.axis_size("rx")
    landed = [both[0]] + [
        shift(both[(x_count - d) % x_count], "rx", (x_count - d) % x_count)
        for d in range(1, x_count)
    ]
    partial_value = jnp.moveaxis(jnp.stack(landed, axis=0), 0, 1)
    partial_value = jnp.where(core == 0, partial_value, partial_value[..., ::-1, :])
    partial_value = jnp.roll(partial_value, lax.axis_index("rx"), axis=1)
    partial_value = jnp.roll(partial_value, lax.axis_index("ry"), axis=2)
    own_part = merged_context
    partial_value = partial_value.reshape(own_part.shape[0], -1)
    tp_count = lax.axis_size("tp")
    block_terms = (
        partial_value.astype(jnp.bfloat16).reshape(-1, tp_count, feature_width).transpose(1, 0, 2)
    )
    own_share = jnp.sum(
        lax.all_to_all(block_terms, "tp", 0, 0, tiled=True).astype(jnp.float32), axis=0
    )
    merged = (merged_residual + layer_scale[None, :] * own_share).astype(jnp.bfloat16)
    merged_count = merged.shape[0]
    counts, starts = request_plan(grid_sizes, image_owner, requests)
    request_ends = starts + counts
    capacity = (IMG_MAX + requests - 1) // requests
    request_ids = jnp.arange(requests, dtype=jnp.int32)
    group_index = jnp.arange(merged_count, dtype=jnp.int32) * requests + device_index
    destination = jnp.sum((request_ends[None, :] <= group_index[:, None]).astype(jnp.int32), axis=1)
    owned_start = jnp.sum(
        jnp.where(destination[:, None] == request_ids[None, :], starts[None, :], 0), axis=1
    )
    target = destination * capacity + (group_index - owned_start) // requests
    usable = destination < requests
    send_slots = jnp.arange(requests * capacity, dtype=jnp.int32)
    placing = ((send_slots[:, None] == target[None, :]) & usable[None, :]).astype(jnp.bfloat16)
    outgoing = jnp.dot(placing, merged, preferred_element_type=jnp.float32).astype(jnp.bfloat16)
    arrived = lax.all_to_all(
        outgoing.reshape(requests, capacity, feature_width),
        REQ,
        split_axis=0,
        concat_axis=0,
        tiled=True,
    )
    arrived = arrived.reshape(requests * capacity, feature_width)
    own_request = request_ids == device_index
    own_count = jnp.sum(jnp.where(own_request, counts, 0))
    own_start = jnp.sum(jnp.where(own_request, starts, 0))
    image_from = image_at[0]
    prompt_count = prompt_len[0]
    seq_slots = prompt.shape[1] + IMG_MAX
    slot_index = jnp.arange(seq_slots, dtype=jnp.int32)
    image_row = slot_index - image_from
    in_image = (image_row >= 0) & (image_row < own_count)
    is_live = slot_index < prompt_count + own_count
    from_prompt = is_live & jnp.logical_not(in_image)
    prompt_row = jnp.where(slot_index < image_from, slot_index, slot_index - own_count)
    prompt_ids = jnp.arange(prompt.shape[1], dtype=jnp.int32)
    prompt_pick = ((prompt_row[:, None] == prompt_ids[None, :]) & from_prompt[:, None]).astype(
        jnp.bfloat16
    )
    full_image = gather_features(arrived, tp_count)
    full_prompt = lax.all_gather(prompt[0], "tp", axis=1, tiled=True)
    full_weight = lax.all_gather(qkv_weight, REQ, axis=0, tiled=True)
    cosine_table, sine_table = rope_tables(seq_slots)
    prompt_rows = jnp.dot(prompt_pick, full_prompt, preferred_element_type=jnp.float32)
    prompt_normed = normalize(prompt_rows.astype(jnp.bfloat16), norm_gain)
    prompt_out = apply_rope(
        jnp.dot(prompt_normed, full_weight, preferred_element_type=jnp.float32),
        cosine_table,
        sine_table,
    ).astype(jnp.bfloat16)
    image_ids = jnp.arange(IMG_MAX, dtype=jnp.int32)
    image_flat = (own_start + image_ids) % requests * capacity + image_ids // requests
    image_order = (
        (image_flat[:, None] == send_slots[None, :]) & (image_ids < own_count)[:, None]
    ).astype(jnp.bfloat16)
    full_image, prompt_out = lax.optimization_barrier((full_image, prompt_out))
    image_rows = jnp.dot(image_order, full_image, preferred_element_type=jnp.float32)
    image_normed = normalize(image_rows.astype(jnp.bfloat16), norm_gain)
    image_out = apply_rope(
        jnp.dot(image_normed, full_weight, preferred_element_type=jnp.float32),
        lax.dynamic_slice_in_dim(cosine_table, image_from, IMG_MAX, 0),
        lax.dynamic_slice_in_dim(sine_table, image_from, IMG_MAX, 0),
    ).astype(jnp.bfloat16)
    image_place = ((image_row[:, None] == image_ids[None, :]) & in_image[:, None]).astype(
        jnp.bfloat16
    )
    placed = jnp.dot(image_place, image_out, preferred_element_type=jnp.float32)
    return jnp.where(in_image[:, None], placed.astype(jnp.bfloat16), prompt_out)


def solution(mesh):
    in_specs = (
        P("req", "tp"),
        P("req", "tp"),
        P("tp", "req"),
        P("tp"),
        P("req", None, "tp"),
        P("req"),
        P("req"),
        P(),
        P(),
        P(),
        P("req", "tp"),
    )
    out_specs = P("req", "tp")
    rows, columns = mesh.devices.shape
    x_size = len({device.coords[0] for device in mesh.devices.flat})
    split_mesh = Mesh(mesh.devices.reshape(x_size, rows // (2 * x_size), 2, columns), REQ + ("tp",))
    rename = lambda spec: P(*(REQ if axis == "req" else axis for axis in spec))
    return jax.shard_map(
        shards,
        mesh=split_mesh,
        in_specs=tuple((rename(spec) for spec in in_specs)),
        out_specs=rename(out_specs),
        check_vma=False,
    )
```

profile of v0, /device:TPU:1, one launch (start us, length us, event | category | flops | bytes accessed | tf_op | source)
XLA Modules:
  0.0 181.3 jit_solution(1262390514091334798)
XLA Ops:
  6.5 0.7 all-gather.6.cloned.1.call-update
  7.3 0.7 all-gather.4.cloned.1.call-update
  8.0 5.9 %collective-permute-start.4 = (bf16[512,64]{0,1:T(8,128)(2,1)}, bf16[512,64]{0,1:T(8,128)(2,1)S(1)}, u32[]{:S(2)}, u32[]{:S(2)}) collective-permute-start(bf16[512,64]{0,1:T(8,128)(2,1)} %param.13), channel_id=1, source_target_pairs={{0,112},{16,0},{32,16},{48,32},{64,48},{80,64},{96,80},{112,96},{1... | collective-permute-start | bytes 196616 | tf_op jit(solution)/shard_map/ppermute | solution.py:63
  13.9 1.9 %collective-permute-start.5 = (bf16[512,64]{0,1:T(8,128)(2,1)}, bf16[512,64]{0,1:T(8,128)(2,1)S(1)}, u32[]{:S(2)}, u32[]{:S(2)}) collective-permute-start(bf16[512,64]{0,1:T(8,128)(2,1)} %param.13), channel_id=1, source_target_pairs={{0,16},{16,32},{32,48},{48,64},{64,80},{80,96},{96,112},{112,0},{1... | collective-permute-start | bytes 196616 | tf_op jit(solution)/shard_map/ppermute | solution.py:63
  15.9 1.4 reshape.242
  17.2 0.6 reduce_sum.96
  17.9 6.8 %collective-permute-start = (bf16[128,512]{1,0:T(8,128)(2,1)S(1)}, bf16[128,512]{1,0:T(8,128)(2,1)S(1)}, u32[]{:S(2)}, u32[]{:S(2)}) collective-permute-start(bf16[128,512]{1,0:T(8,128)(2,1)S(1)} %multiply_convert_fusion.2), channel_id=1, source_target_pairs={{0,8},{8,0},{1,9},{9,1},{2,10},{10,2},{3,11},{11,3},{4,12},{12,4},... | collective-permute-start | bytes 393224 | tf_op jit(solution)/shard_map/ppermute | solution.py:121
  24.8 1.9 %collective-permute-start.6 = (bf16[3,512,64]{1,2,0:T(8,128)(2,1)S(1)}, bf16[3,512,64]{1,2,0:T(8,128)(2,1)S(1)}, u32[]{:S(2)}, u32[]{:S(2)}) collective-permute-start(bf16[3,512,64]{1,2,0:T(8,128)(2,1)S(1)} %pad_maximum_fusion.3), channel_id=1, source_target_pairs={{0,80},{16,96},{32,112},{48,0},{64,16},{80,32},{96,48},{112,64},{1... | collective-permute-start | bytes 589832 | tf_op jit(solution)/shard_map/ppermute | solution.py:63
  26.7 5.2 %collective-permute-start.7 = (bf16[3,512,64]{1,2,0:T(8,128)(2,1)S(1)}, bf16[3,512,64]{1,2,0:T(8,128)(2,1)S(1)}, u32[]{:S(2)}, u32[]{:S(2)}) collective-permute-start(bf16[3,512,64]{1,2,0:T(8,128)(2,1)S(1)} %pad_maximum_fusion.3), channel_id=1, source_target_pairs={{0,48},{16,64},{32,80},{48,96},{64,112},{80,0},{96,16},{112,32},{1... | collective-permute-start | bytes 589832 | tf_op jit(solution)/shard_map/ppermute | solution.py:63
  32.0 1.9 %collective-permute-start.1 = (bf16[2,128,512]{2,1,0:T(8,128)(2,1)S(1)}, bf16[2,128,512]{2,1,0:T(8,128)(2,1)S(1)}, u32[]{:S(2)}, u32[]{:S(2)}) collective-permute-start(bf16[2,128,512]{2,1,0:T(8,128)(2,1)S(1)} %get-tuple-element.24), channel_id=1, source_target_pairs={{0,384},{128,0},{256,128},{384,256},{1,385},{129,1},{257,129},{385... | collective-permute-start | bytes 786440 | tf_op jit(solution)/shard_map/ppermute | solution.py:63
  33.9 1.9 %collective-permute-start.2 = (bf16[2,128,512]{2,1,0:T(8,128)(2,1)S(1)}, bf16[2,128,512]{2,1,0:T(8,128)(2,1)S(1)}, u32[]{:S(2)}, u32[]{:S(2)}) collective-permute-start(bf16[2,128,512]{2,1,0:T(8,128)(2,1)S(1)} %get-tuple-element.24), channel_id=1, source_target_pairs={{0,256},{128,384},{256,0},{384,128},{1,257},{129,385},{257,1},{385... | collective-permute-start | bytes 786440 | tf_op jit(solution)/shard_map/ppermute | solution.py:63
  35.8 3.4 %collective-permute-start.3 = (bf16[2,128,512]{2,1,0:T(8,128)(2,1)S(1)}, bf16[2,128,512]{2,1,0:T(8,128)(2,1)S(1)}, u32[]{:S(2)}, u32[]{:S(2)}) collective-permute-start(bf16[2,128,512]{2,1,0:T(8,128)(2,1)S(1)} %get-tuple-element.24), channel_id=1, source_target_pairs={{0,128},{128,256},{256,384},{384,0},{1,129},{129,257},{257,385},{3... | collective-permute-start | bytes 786440 | tf_op jit(solution)/shard_map/ppermute | solution.py:63
  39.2 7.2 %collective-permute-done.7 = bf16[3,512,64]{1,2,0:T(8,128)(2,1)S(1)} collective-permute-done((bf16[3,512,64]{1,2,0:T(8,128)(2,1)S(1)}, bf16[3,512,64]{1,2,0:T(8,128)(2,1)S(1)}, u32[]{:S(2)}, u32[]{:S(2)}) %collective-permute-start.7) | collective-permute-done | bytes 196640 | tf_op jit(solution)/shard_map/ppermute | solution.py:63
  46.5 4.8 %collective-permute-done.3 = bf16[2,128,512]{2,1,0:T(8,128)(2,1)S(1)} collective-permute-done((bf16[2,128,512]{2,1,0:T(8,128)(2,1)S(1)}, bf16[2,128,512]{2,1,0:T(8,128)(2,1)S(1)}, u32[]{:S(2)}, u32[]{:S(2)}) %collective-permute-start.3) | collective-permute-done | bytes 262176 | tf_op jit(solution)/shard_map/ppermute | solution.py:63
  51.2 0.7 convolution_convert_fusion.2
  52.1 2.3 %collective-permute-start.8 = (bf16[4,128,8,64]{1,3,2,0:T(8,128)(2,1)S(1)}, bf16[4,128,8,64]{1,3,2,0:T(8,128)(2,1)S(1)}, u32[]{:S(2)}, u32[]{:S(2)}) collective-permute-start(bf16[4,128,8,64]{1,3,2,0:T(8,128)(2,1)S(1)} %get-tuple-element.20), channel_id=1, source_target_pairs={{0,8},{8,0},{1,9},{9,1},{2,10},{10,2},{3,11},{11,3},{4,12},{12,4},... | collective-permute-start | bytes 1572872 | tf_op jit(solution)/shard_map/ppermute | solution.py:131
  54.4 1.5 collective-permute-done.8
  56.0 2.2 %collective-permute-start.9 = (bf16[128,8,2,64]{0,3,1,2:T(8,128)(2,1)S(1)}, bf16[128,8,2,64]{0,3,1,2:T(8,128)(2,1)S(1)}, u32[]{:S(2)}, u32[]{:S(2)}) collective-permute-start(bf16[128,8,2,64]{0,3,1,2:T(8,128)(2,1)S(1)} %get-tuple-element.16), channel_id=1, source_target_pairs={{0,384},{128,0},{256,128},{384,256},{1,385},{129,1},{257,129},{385... | collective-permute-start | bytes 786440 | tf_op jit(solution)/shard_map/ppermute | solution.py:63
  58.2 1.9 %collective-permute-start.10 = (bf16[128,8,2,64]{0,3,1,2:T(8,128)(2,1)S(1)}, bf16[128,8,2,64]{0,3,1,2:T(8,128)(2,1)S(1)}, u32[]{:S(2)}, u32[]{:S(2)}) collective-permute-start(bf16[128,8,2,64]{0,3,1,2:T(8,128)(2,1)S(1)} %get-tuple-element.18), channel_id=1, source_target_pairs={{0,256},{128,384},{256,0},{384,128},{1,257},{129,385},{257,1},{385... | collective-permute-start | bytes 786440 | tf_op jit(solution)/shard_map/ppermute | solution.py:63
  60.1 3.1 %collective-permute-start.11 = (bf16[128,8,2,64]{0,3,1,2:T(8,128)(2,1)S(1)}, bf16[128,8,2,64]{0,3,1,2:T(8,128)(2,1)S(1)}, u32[]{:S(2)}, u32[]{:S(2)}) collective-permute-start(bf16[128,8,2,64]{0,3,1,2:T(8,128)(2,1)S(1)} %get-tuple-element.17), channel_id=1, source_target_pairs={{0,128},{128,256},{256,384},{384,0},{1,129},{129,257},{257,385},{3... | collective-permute-start | bytes 786440 | tf_op jit(solution)/shard_map/ppermute | solution.py:63
  63.2 2.2 %collective-permute-done.9 = bf16[128,8,2,64]{0,3,1,2:T(8,128)(2,1)S(1)} collective-permute-done((bf16[128,8,2,64]{0,3,1,2:T(8,128)(2,1)S(1)}, bf16[128,8,2,64]{0,3,1,2:T(8,128)(2,1)S(1)}, u32[]{:S(2)}, u32[]{:S(2)}) %collective-permute-start.9) | collective-permute-done | bytes 262176 | tf_op jit(solution)/shard_map/ppermute | solution.py:63
  65.4 3.4 %collective-permute-done.10 = bf16[128,8,2,64]{0,3,1,2:T(8,128)(2,1)S(1)} collective-permute-done((bf16[128,8,2,64]{0,3,1,2:T(8,128)(2,1)S(1)}, bf16[128,8,2,64]{0,3,1,2:T(8,128)(2,1)S(1)}, u32[]{:S(2)}, u32[]{:S(2)}) %collective-permute-start.10) | collective-permute-done | bytes 262176 | tf_op jit(solution)/shard_map/ppermute | solution.py:63
  68.8 6.6 %collective-permute-done.11 = bf16[128,8,2,64]{0,3,1,2:T(8,128)(2,1)S(1)} collective-permute-done((bf16[128,8,2,64]{0,3,1,2:T(8,128)(2,1)S(1)}, bf16[128,8,2,64]{0,3,1,2:T(8,128)(2,1)S(1)}, u32[]{:S(2)}, u32[]{:S(2)}) %collective-permute-start.11) | collective-permute-done | bytes 262176 | tf_op jit(solution)/shard_map/ppermute | solution.py:63
  75.9 0.4 fusion.12
  76.3 0.4 fusion.11
  76.7 1.1 copy.43
  77.8 8.6 %all-to-all-start = ((bf16[8,128,512]{1,2,0:T(8,128)(2,1)}), bf16[8,128,512]{1,2,0:T(8,128)(2,1)S(1)}, u32[]{:S(2)}, u32[]{:S(2)}) async-start(bf16[8,128,512]{1,2,0:T(8,128)(2,1)} %bitcast.27), calls=%async_computation | async-start | bytes 2097152 | tf_op jit(solution)/shard_map/all_to_all | solution.py:149
  88.2 0.3 reshape.240
  88.5 0.6 reduce_sum.95
  89.2 0.7 fusion.52
  90.6 0.7 fusion.49
  91.3 0.7 subtract_select_fusion
  92.2 0.4 fusion.38
  92.6 23.0 %all-to-all-done = bf16[8,128,512]{1,2,0:T(8,128)(2,1)S(1)} async-done(((bf16[8,128,512]{1,2,0:T(8,128)(2,1)}), bf16[8,128,512]{1,2,0:T(8,128)(2,1)S(1)}, u32[]{:S(2)}, u32[]{:S(2)}) %all-to-all-start) | async-done | bytes 1048608 | tf_op jit(solution)/shard_map/all_to_all | solution.py:149
  116.1 0.7 reshape.235
  116.9 7.3 %all-to-all-start.1 = ((bf16[64,2,512]{2,1,0:T(2,128)(2,1)}), bf16[64,2,512]{2,1,0:T(2,128)(2,1)S(1)}, u32[]{:S(2)}, u32[]{:S(2)}) async-start(bf16[64,2,512]{2,1,0:T(2,128)(2,1)} %reshape.235), calls=%async_computation.1 | async-start | bytes 262144 | tf_op jit(solution)/shard_map/all_to_all | solution.py:167
  124.2 0.7 iota_compare_fusion.8
  125.0 9.8 %all-to-all-done.1 = bf16[64,2,512]{2,1,0:T(2,128)(2,1)S(1)} async-done(((bf16[64,2,512]{2,1,0:T(2,128)(2,1)}), bf16[64,2,512]{2,1,0:T(2,128)(2,1)S(1)}, u32[]{:S(2)}, u32[]{:S(2)}) %all-to-all-start.1) | async-done | bytes 131104 | tf_op jit(solution)/shard_map/all_to_all | solution.py:167
  134.9 1.1 broadcast_in_dim.28
  136.1 3.7 %all-to-all-start.2 = ((bf16[8,128,512]{1,2,0:T(8,128)(2,1)}), bf16[8,128,512]{1,2,0:T(8,128)(2,1)S(1)}, u32[]{:S(2)}, u32[]{:S(2)}) async-start(bf16[8,128,512]{1,2,0:T(8,128)(2,1)} %broadcast_in_dim.28), calls=%async_computation.2 | async-start | bytes 2097152 | tf_op jit(solution)/shard_map/all_to_all | solution.py:57
  139.8 0.6 fusion.50
  140.5 4.4 %fusion = (f32[384]{0:T(512)S(1)}, bf16[384,4096]{1,0:T(8,128)(2,1)}) fusion(bf16[1,256,4096]{2,1,0:T(8,128)(2,1)} %all-gather.6.cloned.1.call-done, s32[384]{0:T(512)S(1)} %subtract_select_fusion, pred[384]{0:T(512)(128)(4,1)S(1)} %get-tuple-element.11), kind=kOutput, calls=%fused_computation.2 | convolution fusion | flops 811794048 | bytes 5246336 | tf_op jit(solution)/shard_map/dot_general | solution.py:195
  144.9 4.5 %all-gather.4.cloned.1.call-done = bf16[4096,768]{1,0:T(8,128)(2,1)} async-done(((bf16[64,768]{1,0:T(8,128)(2,1)}), bf16[4096,768]{1,0:T(8,128)(2,1)}) %all-gather.4.cloned.1.call-update) | async-done | bytes 6291472 | tf_op jit(solution)/shard_map/all_gather | solution.py:193
  149.4 6.7 %fusion.4 = f32[384,768]{0,1:T(8,128)S(1)} fusion(bf16[4096,768]{1,0:T(8,128)(2,1)} %all-gather.4.cloned.1.call-done, bf16[384,4096]{1,0:T(8,128)(2,1)} %get-tuple-element.29, f32[4096]{0:T(1024)S(1)} %copy-done.2, f32[384]{0:T(512)S(1)} %add_rsqrt_fusion), kind=kOutput, calls=%fused_computation.8 | convolution fusion | flops 2422210560 | bytes 10634752 | tf_op jit(solution)/shard_map/dot_general | solution.py:198
  156.3 10.5 %all-to-all-done.2 = bf16[8,128,512]{1,2,0:T(8,128)(2,1)S(1)} async-done(((bf16[8,128,512]{1,2,0:T(8,128)(2,1)}), bf16[8,128,512]{1,2,0:T(8,128)(2,1)S(1)}, u32[]{:S(2)}, u32[]{:S(2)}) %all-to-all-start.2) | async-done | bytes 1048608 | tf_op jit(solution)/shard_map/all_to_all | solution.py:57
  166.9 0.6 multiply_reduce_fusion
  167.4 5.4 %fusion.10 = f32[128,768]{0,1:T(8,128)S(1)} fusion(bf16[4096,768]{1,0:T(8,128)(2,1)} %all-gather.4.cloned.1.call-done, f32[128,4096]{1,0:T(8,128)S(1)} %get-tuple-element.31, f32[4096]{0:T(1024)S(1)} %copy-done.2, f32[128]{0:T(128)S(1)} %add_rsqrt_fusion.1), kind=kOutput, calls=%fused_computation.30 | convolution fusion | flops 806879232 | bytes 8798720 | tf_op jit(solution)/shard_map/dot_general | solution.py:211
  173.2 1.2 fusion.9
  (61 shorter events, 2.8 us)
Async XLA Ops:
  6.5 18.2 %copy-start.1 = (bf16[512,64]{0,1:T(8,128)(2,1)S(1)}, bf16[512,64]{0,1:T(8,128)(2,1)}, u32[]{:S(2)}) copy-start(bf16[512,64]{0,1:T(8,128)(2,1)} %param.13) | copy-start | bytes 196612
  6.5 134.0 %all-gather.6.cloned.1.call-start = ((), (), s32[]{:S(2)}) async-start(), calls=%async_computation.4 | async-start | bytes 2359296 | tf_op jit(solution)/shard_map/all_gather | solution.py:192
  7.3 142.1 %all-gather.4.cloned.1.call-start = ((), (), s32[]{:S(2)}) async-start(), calls=%async_computation.3 | async-start | bytes 6389760 | tf_op jit(solution)/shard_map/all_gather | solution.py:193
  8.0 16.7 %collective-permute-start.4 = (bf16[512,64]{0,1:T(8,128)(2,1)}, bf16[512,64]{0,1:T(8,128)(2,1)S(1)}, u32[]{:S(2)}, u32[]{:S(2)}) collective-permute-start(bf16[512,64]{0,1:T(8,128)(2,1)} %param.13), channel_id=1, source_target_pairs={{0,112},{16,0},{32,16},{48,32},{64,48},{80,64},{96,80},{112,96},{1... | collective-permute-start | bytes 196616 | tf_op jit(solution)/shard_map/ppermute | solution.py:63
  13.9 10.8 %collective-permute-start.5 = (bf16[512,64]{0,1:T(8,128)(2,1)}, bf16[512,64]{0,1:T(8,128)(2,1)S(1)}, u32[]{:S(2)}, u32[]{:S(2)}) collective-permute-start(bf16[512,64]{0,1:T(8,128)(2,1)} %param.13), channel_id=1, source_target_pairs={{0,16},{16,32},{32,48},{48,64},{64,80},{80,96},{96,112},{112,0},{1... | collective-permute-start | bytes 196616 | tf_op jit(solution)/shard_map/ppermute | solution.py:63
  17.9 14.0 %collective-permute-start = (bf16[128,512]{1,0:T(8,128)(2,1)S(1)}, bf16[128,512]{1,0:T(8,128)(2,1)S(1)}, u32[]{:S(2)}, u32[]{:S(2)}) collective-permute-start(bf16[128,512]{1,0:T(8,128)(2,1)S(1)} %multiply_convert_fusion.2), channel_id=1, source_target_pairs={{0,8},{8,0},{1,9},{9,1},{2,10},{10,2},{3,11},{11,3},{4,12},{12,4},... | collective-permute-start | bytes 393224 | tf_op jit(solution)/shard_map/ppermute | solution.py:121
  24.8 14.4 %collective-permute-start.6 = (bf16[3,512,64]{1,2,0:T(8,128)(2,1)S(1)}, bf16[3,512,64]{1,2,0:T(8,128)(2,1)S(1)}, u32[]{:S(2)}, u32[]{:S(2)}) collective-permute-start(bf16[3,512,64]{1,2,0:T(8,128)(2,1)S(1)} %pad_maximum_fusion.3), channel_id=1, source_target_pairs={{0,80},{16,96},{32,112},{48,0},{64,16},{80,32},{96,48},{112,64},{1... | collective-permute-start | bytes 589832 | tf_op jit(solution)/shard_map/ppermute | solution.py:63
  26.7 19.7 %collective-permute-start.7 = (bf16[3,512,64]{1,2,0:T(8,128)(2,1)S(1)}, bf16[3,512,64]{1,2,0:T(8,128)(2,1)S(1)}, u32[]{:S(2)}, u32[]{:S(2)}) collective-permute-start(bf16[3,512,64]{1,2,0:T(8,128)(2,1)S(1)} %pad_maximum_fusion.3), channel_id=1, source_target_pairs={{0,48},{16,64},{32,80},{48,96},{64,112},{80,0},{96,16},{112,32},{1... | collective-permute-start | bytes 589832 | tf_op jit(solution)/shard_map/ppermute | solution.py:63
  32.0 14.5 %collective-permute-start.1 = (bf16[2,128,512]{2,1,0:T(8,128)(2,1)S(1)}, bf16[2,128,512]{2,1,0:T(8,128)(2,1)S(1)}, u32[]{:S(2)}, u32[]{:S(2)}) collective-permute-start(bf16[2,128,512]{2,1,0:T(8,128)(2,1)S(1)} %get-tuple-element.24), channel_id=1, source_target_pairs={{0,384},{128,0},{256,128},{384,256},{1,385},{129,1},{257,129},{385... | collective-permute-start | bytes 786440 | tf_op jit(solution)/shard_map/ppermute | solution.py:63
  33.9 12.6 %collective-permute-start.2 = (bf16[2,128,512]{2,1,0:T(8,128)(2,1)S(1)}, bf16[2,128,512]{2,1,0:T(8,128)(2,1)S(1)}, u32[]{:S(2)}, u32[]{:S(2)}) collective-permute-start(bf16[2,128,512]{2,1,0:T(8,128)(2,1)S(1)} %get-tuple-element.24), channel_id=1, source_target_pairs={{0,256},{128,384},{256,0},{384,128},{1,257},{129,385},{257,1},{385... | collective-permute-start | bytes 786440 | tf_op jit(solution)/shard_map/ppermute | solution.py:63
  35.8 15.4 %collective-permute-start.3 = (bf16[2,128,512]{2,1,0:T(8,128)(2,1)S(1)}, bf16[2,128,512]{2,1,0:T(8,128)(2,1)S(1)}, u32[]{:S(2)}, u32[]{:S(2)}) collective-permute-start(bf16[2,128,512]{2,1,0:T(8,128)(2,1)S(1)} %get-tuple-element.24), channel_id=1, source_target_pairs={{0,128},{128,256},{256,384},{384,0},{1,129},{129,257},{257,385},{3... | collective-permute-start | bytes 786440 | tf_op jit(solution)/shard_map/ppermute | solution.py:63
  52.1 3.8 %collective-permute-start.8 = (bf16[4,128,8,64]{1,3,2,0:T(8,128)(2,1)S(1)}, bf16[4,128,8,64]{1,3,2,0:T(8,128)(2,1)S(1)}, u32[]{:S(2)}, u32[]{:S(2)}) collective-permute-start(bf16[4,128,8,64]{1,3,2,0:T(8,128)(2,1)S(1)} %get-tuple-element.20), channel_id=1, source_target_pairs={{0,8},{8,0},{1,9},{9,1},{2,10},{10,2},{3,11},{11,3},{4,12},{12,4},... | collective-permute-start | bytes 1572872 | tf_op jit(solution)/shard_map/ppermute | solution.py:131
  56.0 9.4 %collective-permute-start.9 = (bf16[128,8,2,64]{0,3,1,2:T(8,128)(2,1)S(1)}, bf16[128,8,2,64]{0,3,1,2:T(8,128)(2,1)S(1)}, u32[]{:S(2)}, u32[]{:S(2)}) collective-permute-start(bf16[128,8,2,64]{0,3,1,2:T(8,128)(2,1)S(1)} %get-tuple-element.16), channel_id=1, source_target_pairs={{0,384},{128,0},{256,128},{384,256},{1,385},{129,1},{257,129},{385... | collective-permute-start | bytes 786440 | tf_op jit(solution)/shard_map/ppermute | solution.py:63
  58.2 10.6 %collective-permute-start.10 = (bf16[128,8,2,64]{0,3,1,2:T(8,128)(2,1)S(1)}, bf16[128,8,2,64]{0,3,1,2:T(8,128)(2,1)S(1)}, u32[]{:S(2)}, u32[]{:S(2)}) collective-permute-start(bf16[128,8,2,64]{0,3,1,2:T(8,128)(2,1)S(1)} %get-tuple-element.18), channel_id=1, source_target_pairs={{0,256},{128,384},{256,0},{384,128},{1,257},{129,385},{257,1},{385... | collective-permute-start | bytes 786440 | tf_op jit(solution)/shard_map/ppermute | solution.py:63
  60.1 15.3 %collective-permute-start.11 = (bf16[128,8,2,64]{0,3,1,2:T(8,128)(2,1)S(1)}, bf16[128,8,2,64]{0,3,1,2:T(8,128)(2,1)S(1)}, u32[]{:S(2)}, u32[]{:S(2)}) collective-permute-start(bf16[128,8,2,64]{0,3,1,2:T(8,128)(2,1)S(1)} %get-tuple-element.17), channel_id=1, source_target_pairs={{0,128},{128,256},{256,384},{384,0},{1,129},{129,257},{257,385},{3... | collective-permute-start | bytes 786440 | tf_op jit(solution)/shard_map/ppermute | solution.py:63
  76.7 9.8 %copy-start.4 = (s32[128,2]{0,1:T(2,128)S(1)}, s32[128,2]{0,1:T(2,128)}, u32[]{:S(2)}) copy-start(s32[128,2]{0,1:T(2,128)} %param.18) | copy-start | bytes 3076
  76.7 9.8 %copy-start.5 = (s32[128]{0:T(128)S(1)}, s32[128]{0:T(128)}, u32[]{:S(2)}) copy-start(s32[128]{0:T(128)} %param.19) | copy-start | bytes 1540
  76.7 11.5 %copy-start = (bf16[512,512]{1,0:T(8,128)(2,1)S(1)}, bf16[512,512]{1,0:T(8,128)(2,1)}, u32[]{:S(2)}) copy-start(bf16[512,512]{1,0:T(8,128)(2,1)} %param.12) | copy-start | bytes 1572868
  77.8 37.9 %all-to-all-start = ((bf16[8,128,512]{1,2,0:T(8,128)(2,1)}), bf16[8,128,512]{1,2,0:T(8,128)(2,1)S(1)}, u32[]{:S(2)}, u32[]{:S(2)}) async-start(bf16[8,128,512]{1,2,0:T(8,128)(2,1)} %bitcast.27), calls=%async_computation | async-start | bytes 2097152 | tf_op jit(solution)/shard_map/all_to_all | solution.py:149
  88.2 27.8 %copy-start.3 = (f32[512]{0:T(512)S(1)}, f32[512]{0:T(512)}, u32[]{:S(2)}) copy-start(f32[512]{0:T(512)} %param.14) | copy-start | bytes 6148
  116.9 17.9 %all-to-all-start.1 = ((bf16[64,2,512]{2,1,0:T(2,128)(2,1)}), bf16[64,2,512]{2,1,0:T(2,128)(2,1)S(1)}, u32[]{:S(2)}, u32[]{:S(2)}) async-start(bf16[64,2,512]{2,1,0:T(2,128)(2,1)} %reshape.235), calls=%async_computation.1 | async-start | bytes 262144 | tf_op jit(solution)/shard_map/all_to_all | solution.py:167
  136.1 30.8 %all-to-all-start.2 = ((bf16[8,128,512]{1,2,0:T(8,128)(2,1)}), bf16[8,128,512]{1,2,0:T(8,128)(2,1)S(1)}, u32[]{:S(2)}, u32[]{:S(2)}) async-start(bf16[8,128,512]{1,2,0:T(8,128)(2,1)} %broadcast_in_dim.28), calls=%async_computation.2 | async-start | bytes 2097152 | tf_op jit(solution)/shard_map/all_to_all | solution.py:57
  140.5 8.9 %copy-start.2 = (f32[4096]{0:T(1024)S(1)}, f32[4096]{0:T(1024)}, u32[]{:S(2)}) copy-start(f32[4096]{0:T(1024)} %param.20) | copy-start | bytes 49156
Sparse Core Ops, SparseCore 0:
  9.4 46.0 all-gather.5
  58.9 90.4 all-gather.3
where the time goes:
time: 182 us; the launch traced here: 181 us
  waiting for transfers between devices  74.9 us (41%)
  starting transfers between devices  58.1 us (32%)
  matrix products  19.2 us (11%)
  between operations  16 us (9%)
  other arithmetic  7.43 us (4%)
  local copies, waits for them, and re-layouts  5.56 us (3%)
    ppermute x10, starting transfers between devices, shift(): lax.ppermute(value, axis, [(k, (k + step) % size) for k in range(size)])  29.3 us
    ppermute x10, waiting for transfers between devices, shift(): lax.ppermute(value, axis, [(k, (k + step) % size) for k in range(size)])  24.2 us
    all_to_all x1, waiting for transfers between devices, shards(): lax.all_to_all(block_terms, 'tp', 0, 0, tiled=True).astype(jnp.float32)  23 us
    all_to_all x1, waiting for transfers between devices, gather_features(): blocks = lax.all_to_all(copies, 'tp', 0, 0, tiled=True)  10.5 us
    all_to_all x1, waiting for transfers between devices, shards(): lax.all_to_all(outgoing.reshape(requests, capacity, feature_width), REQ,...  9.79 us
    all_to_all x1, starting transfers between devices, shards(): lax.all_to_all(block_terms, 'tp', 0, 0, tiled=True).astype(jnp.float32)  8.64 us
    all_to_all x1, starting transfers between devices, shards(): lax.all_to_all(outgoing.reshape(requests, capacity, feature_width), REQ,...  7.3 us
    ppermute x1, starting transfers between devices, shards(): lax.ppermute(merged_context, 'rc', swap)  6.78 us
  transfers between devices with their start and end apart: 17, of which 10 were waited for; matrix products, arithmetic and copies ran while one was open for 14% of the time, Pallas kernels for 0%

commit v1 on v0

--- a/solution.py
+++ b/solution.py
@@ -190,7 +190,8 @@
     )
     full_image = gather_features(arrived, tp_count)
     full_prompt = lax.all_gather(prompt[0], "tp", axis=1, tiled=True)
-    full_weight = lax.all_gather(qkv_weight, REQ, axis=0, tiled=True)
+    sent = jnp.stack([qkv_weight] * lax.axis_size(REQ))
+    full_weight = jnp.concatenate(lax.all_to_all(sent, REQ, 0, 0), axis=0)
     cosine_table, sine_table = rope_tables(seq_slots)
     prompt_rows = jnp.dot(prompt_pick, full_prompt, preferred_element_type=jnp.float32)
     prompt_normed = normalize(prompt_rows.astype(jnp.bfloat16), norm_gain)

time: 182 us -> 329 us (1.81)
  waiting for transfers between devices: 74.9 us -> 190 us
  blocking collectives: 0 us -> 20.1 us
  local copies, waits for them, and re-layouts: 5.56 us -> 16.9 us
    all_to_all x1, waiting for transfers between devices: 9.79 us -> 135 us  [shards(): full_weight = jnp.concatenate(lax.all_to_all(sent, REQ, 0, 0), axis=0)]
    all_to_all x0 -> x1, blocking collectives: none -> 20.1 us  [shards(): lax.all_to_all(outgoing.reshape(requests, capacity, feature_width), REQ,...]
    dot_general x0 -> x1, local copies, waits for them, and re-layouts: none -> 8.64 us  [shards(): jnp.dot(prompt_normed, full_weight, preferred_element_type=jnp.float32)]
    ppermute x10, waiting for transfers between devices: 24.2 us -> 19.1 us  [shift(): lax.ppermute(value, axis, [(k, (k + step) % size) for k in range(size)])]
    all_gather x1 -> x0, waiting for transfers between devices: 4.49 us -> none  [shards(): full_weight = lax.all_gather(qkv_weight, REQ, axis=0, tiled=True)]
    all_to_all x1, waiting for transfers between devices: 10.5 us -> 6.59 us  [gather_features(): blocks = lax.all_to_all(copies, 'tp', 0, 0, tiled=True)]
    all_to_all x1, waiting for transfers between devices: 23 us -> 26.8 us  [shards(): lax.all_to_all(block_terms, 'tp', 0, 0, tiled=True).astype(jnp.float32)]
    another operation x1 -> x2, local copies, waits for them, and re-layouts: 0.1 us -> 3.51 us  [the longest x1 3.42 us: shards(): sent = jnp.stack([qkv_weight] * lax.axis_size(REQ))]
  transfers between devices with their start and end apart: 17 -> 16, of which waited for: 10 -> 10; matrix products, arithmetic and copies ran while one was open for 14% -> 9% of each run, Pallas kernels for 0% -> 0%
where the time goes in v1:
time: 329 us; the launch traced here: 327 us
  waiting for transfers between devices  190 us (58%)
  starting transfers between devices  58.5 us (18%)
  blocking collectives  20.1 us (6%)
  matrix products  18.3 us (6%)
  local copies, waits for them, and re-layouts  16.9 us (5%)
  between operations  15.9 us (5%)
  other arithmetic  7.26 us (2%)
    all_to_all x1, waiting for transfers between devices, shards(): full_weight = jnp.concatenate(lax.all_to_all(sent, REQ, 0, 0), axis=0)  135 us
    ppermute x10, starting transfers between devices, shift(): lax.ppermute(value, axis, [(k, (k + step) % size) for k in range(size)])  32.7 us
    all_to_all x1, waiting for transfers between devices, shards(): lax.all_to_all(block_terms, 'tp', 0, 0, tiled=True).astype(jnp.float32)  26.8 us
    all_to_all x1, blocking collectives, shards(): lax.all_to_all(outgoing.reshape(requests, capacity, feature_width), REQ,...  20.1 us
    ppermute x10, waiting for transfers between devices, shift(): lax.ppermute(value, axis, [(k, (k + step) % size) for k in range(size)])  19.1 us
    dot_general x1, local copies, waits for them, and re-layouts, shards(): jnp.dot(prompt_normed, full_weight, preferred_element_type=jnp.float32)  8.64 us
    ppermute x1, starting transfers between devices, shards(): lax.ppermute(merged_context, 'rc', swap)  6.78 us
    dot_general x1, matrix products, shards(): jnp.dot(prompt_normed, full_weight, preferred_element_type=jnp.float32)  6.66 us
  transfers between devices with their start and end apart: 16, of which 10 were waited for; matrix products, arithmetic and copies ran while one was open for 9% of the time, Pallas kernels for 0%

profile of v1, /device:TPU:1, one launch (start us, length us, event | category | flops | bytes accessed | tf_op | source)
XLA Modules:
  0.0 326.7 jit_solution(461203441838020194)
XLA Ops:
  6.5 6.0 %collective-permute-start.4 = (bf16[512,64]{0,1:T(8,128)(2,1)}, bf16[512,64]{0,1:T(8,128)(2,1)S(1)}, u32[]{:S(2)}, u32[]{:S(2)}) collective-permute-start(bf16[512,64]{0,1:T(8,128)(2,1)} %param.13), channel_id=1, source_target_pairs={{0,112},{16,0},{32,16},{48,32},{64,48},{80,64},{96,80},{112,96},{1... | collective-permute-start | bytes 196616 | tf_op jit(solution)/shard_map/ppermute | solution.py:63
  12.6 1.9 collective-permute-start.5
  14.5 1.4 reshape.253
  15.9 0.6 reduce_sum.96
  16.5 6.8 %collective-permute-start = (bf16[128,512]{1,0:T(8,128)(2,1)S(1)}, bf16[128,512]{1,0:T(8,128)(2,1)S(1)}, u32[]{:S(2)}, u32[]{:S(2)}) collective-permute-start(bf16[128,512]{1,0:T(8,128)(2,1)S(1)} %multiply_convert_fusion.1), channel_id=1, source_target_pairs={{0,8},{8,0},{1,9},{9,1},{2,10},{10,2},{3,11},{11,3},{4,12},{12,4},... | collective-permute-start | bytes 393224 | tf_op jit(solution)/shard_map/ppermute | solution.py:121
  23.4 1.9 collective-permute-start.6
  25.4 5.2 %collective-permute-start.7 = (bf16[3,512,64]{1,2,0:T(8,128)(2,1)S(1)}, bf16[3,512,64]{1,2,0:T(8,128)(2,1)S(1)}, u32[]{:S(2)}, u32[]{:S(2)}) collective-permute-start(bf16[3,512,64]{1,2,0:T(8,128)(2,1)S(1)} %pad_maximum_fusion.3), channel_id=1, source_target_pairs={{0,48},{16,64},{32,80},{48,96},{64,112},{80,0},{96,16},{112,32},{1... | collective-permute-start | bytes 589832 | tf_op jit(solution)/shard_map/ppermute | solution.py:63
  30.6 1.9 collective-permute-start.3
  32.5 1.9 collective-permute-start.2
  34.5 4.6 %collective-permute-start.1 = (bf16[2,128,512]{2,1,0:T(8,128)(2,1)S(1)}, bf16[2,128,512]{2,1,0:T(8,128)(2,1)S(1)}, u32[]{:S(2)}, u32[]{:S(2)}) collective-permute-start(bf16[2,128,512]{2,1,0:T(8,128)(2,1)S(1)} %get-tuple-element.24), channel_id=1, source_target_pairs={{0,384},{128,0},{256,128},{384,256},{1,385},{129,1},{257,129},{385... | collective-permute-start | bytes 786440 | tf_op jit(solution)/shard_map/ppermute | solution.py:63
  39.1 6.0 %collective-permute-done.7 = bf16[3,512,64]{1,2,0:T(8,128)(2,1)S(1)} collective-permute-done((bf16[3,512,64]{1,2,0:T(8,128)(2,1)S(1)}, bf16[3,512,64]{1,2,0:T(8,128)(2,1)S(1)}, u32[]{:S(2)}, u32[]{:S(2)}) %collective-permute-start.7) | collective-permute-done | bytes 196640 | tf_op jit(solution)/shard_map/ppermute | solution.py:63
  45.1 1.5 collective-permute-done.3
  46.6 2.4 collective-permute-done.1
  49.0 0.7 convolution_convert_fusion.2
  49.9 3.5 %collective-permute-start.8 = (bf16[4,128,8,64]{1,3,2,0:T(8,128)(2,1)S(1)}, bf16[4,128,8,64]{1,3,2,0:T(8,128)(2,1)S(1)}, u32[]{:S(2)}, u32[]{:S(2)}) collective-permute-start(bf16[4,128,8,64]{1,3,2,0:T(8,128)(2,1)S(1)} %get-tuple-element.20), channel_id=1, source_target_pairs={{0,8},{8,0},{1,9},{9,1},{2,10},{10,2},{3,11},{11,3},{4,12},{12,4},... | collective-permute-start | bytes 1572872 | tf_op jit(solution)/shard_map/ppermute | solution.py:131
  53.3 1.5 collective-permute-done.8
  54.9 1.9 collective-permute-start.11
  56.9 5.4 %collective-permute-start.10 = (bf16[128,8,2,64]{0,3,1,2:T(8,128)(2,1)S(1)}, bf16[128,8,2,64]{0,3,1,2:T(8,128)(2,1)S(1)}, u32[]{:S(2)}, u32[]{:S(2)}) collective-permute-start(bf16[128,8,2,64]{0,3,1,2:T(8,128)(2,1)S(1)} %get-tuple-element.18), channel_id=1, source_target_pairs={{0,256},{128,384},{256,0},{384,128},{1,257},{129,385},{257,1},{385... | collective-permute-start | bytes 786440 | tf_op jit(solution)/shard_map/ppermute | solution.py:63
  62.3 1.9 collective-permute-start.9
  64.3 1.3 collective-permute-done.11
  65.6 6.5 %collective-permute-done.10 = bf16[128,8,2,64]{0,3,1,2:T(8,128)(2,1)S(1)} collective-permute-done((bf16[128,8,2,64]{0,3,1,2:T(8,128)(2,1)S(1)}, bf16[128,8,2,64]{0,3,1,2:T(8,128)(2,1)S(1)}, u32[]{:S(2)}, u32[]{:S(2)}) %collective-permute-start.10) | collective-permute-done | bytes 262176 | tf_op jit(solution)/shard_map/ppermute | solution.py:63
  72.0 1.4 collective-permute-done.9
  73.8 0.4 fusion.17
  74.2 0.4 fusion.16
  74.6 1.1 copy.43
  75.7 6.3 %all-to-all-start = ((bf16[8,128,512]{1,2,0:T(8,128)(2,1)}), bf16[8,128,512]{1,2,0:T(8,128)(2,1)S(1)}, u32[]{:S(2)}, u32[]{:S(2)}) async-start(bf16[8,128,512]{1,2,0:T(8,128)(2,1)} %bitcast.27), calls=%async_computation | async-start | bytes 2097152 | tf_op jit(solution)/shard_map/all_to_all | solution.py:149
  82.4 0.6 reduce_sum.95
  83.6 0.7 fusion.57
  84.3 26.8 %all-to-all-done = bf16[8,128,512]{1,2,0:T(8,128)(2,1)S(1)} async-done(((bf16[8,128,512]{1,2,0:T(8,128)(2,1)}), bf16[8,128,512]{1,2,0:T(8,128)(2,1)S(1)}, u32[]{:S(2)}, u32[]{:S(2)}) %all-to-all-start) | async-done | bytes 1048608 | tf_op jit(solution)/shard_map/all_to_all | solution.py:149
  111.7 20.1 %all_to_all.20 = bf16[64,2,512]{2,1,0:T(2,128)(2,1)S(1)} all-to-all(bf16[64,2,512]{2,1,0:T(2,128)(2,1)S(1)} %reshape.246), channel_id=1, replica_groups=mesh['rx'=4,'ry'=8,'rc'=2,'tp'=8] {'rx','ry','rc'}, dimensions={0} | all-to-all | bytes 262144 | tf_op jit(solution)/shard_map/all_to_all | solution.py:167
  131.9 3.4 %stack.57 = bf16[64,64,768]{2,1,0:T(8,128)(2,1)} broadcast(bf16[64,768]{1,0:T(8,128)(2,1)S(1)} %copy-done.2), dimensions={1,2} | broadcast | bytes 6389760 | tf_op jit(solution)/shard_map/stack | solution.py:193
  135.3 5.5 %all-to-all-start.3 = ((bf16[64,64,768]{2,1,0:T(8,128)(2,1)}), bf16[64,64,768]{2,1,0:T(8,128)(2,1)}, u32[]{:S(2)}, u32[]{:S(2)}) async-start(bf16[64,64,768]{2,1,0:T(8,128)(2,1)} %stack.57), calls=%async_computation.3 | async-start | bytes 12582912 | tf_op jit(solution)/shard_map/all_to_all | solution.py:194
  140.8 0.7 all-gather.3.cloned.1.call-update
  143.4 0.6 iota_compare_fusion.8
  144.1 0.7 fusion.55
  144.7 0.6 fusion.54
  145.4 0.6 subtract_select_fusion
  146.0 0.4 fusion.43
  146.7 134.9 %all-to-all-done.3 = bf16[64,64,768]{2,1,0:T(8,128)(2,1)} async-done(((bf16[64,64,768]{2,1,0:T(8,128)(2,1)}), bf16[64,64,768]{2,1,0:T(8,128)(2,1)}, u32[]{:S(2)}, u32[]{:S(2)}) %all-to-all-start.3) | async-done | bytes 6291488 | tf_op jit(solution)/shard_map/all_to_all | solution.py:194
  281.7 1.1 broadcast_in_dim.28
  282.8 3.7 %all-to-all-start.2 = ((bf16[8,128,512]{1,2,0:T(8,128)(2,1)}), bf16[8,128,512]{1,2,0:T(8,128)(2,1)S(1)}, u32[]{:S(2)}, u32[]{:S(2)}) async-start(bf16[8,128,512]{1,2,0:T(8,128)(2,1)} %broadcast_in_dim.28), calls=%async_computation.2 | async-start | bytes 2097152 | tf_op jit(solution)/shard_map/all_to_all | solution.py:57
  286.6 4.3 %fusion = (f32[384]{0:T(512)S(1)}, bf16[384,4096]{1,0:T(8,128)(2,1)}) fusion(bf16[1,256,4096]{2,1,0:T(8,128)(2,1)} %all-gather.3.cloned.1.call-done, s32[384]{0:T(512)S(1)} %subtract_select_fusion, pred[384]{0:T(512)(128)(4,1)S(1)} %get-tuple-element.11), kind=kOutput, calls=%fused_computation.2 | convolution fusion | flops 811794048 | bytes 5246336 | tf_op jit(solution)/shard_map/dot_general | solution.py:196
  290.9 8.6 %copy.46 = bf16[768,4096]{1,0:T(8,128)(2,1)} copy(bf16[768,4096]{0,1:T(8,128)(2,1)} %bitcast.34) | data formatting | bytes 12582912 | tf_op jit(solution)/shard_map/dot_general | solution.py:199
  299.5 6.7 %fusion.10 = f32[384,1,6,128]{0,3,2,1:T(8,128)S(1)} fusion(bf16[6,128,4096]{2,1,0:T(8,128)(2,1)} %bitcast.93, bf16[384,4096]{1,0:T(8,128)(2,1)} %get-tuple-element.29, f32[4096]{0:T(1024)S(1)} %copy-done.3, f32[384]{0:T(512)S(1)} %add_rsqrt_fusion), kind=kOutput, calls=%fused_computation.22 | convolution fusion | flops 2422210560 | bytes 10634752 | tf_op jit(solution)/shard_map/dot_general | solution.py:199
  306.4 6.6 %all-to-all-done.2 = bf16[8,128,512]{1,2,0:T(8,128)(2,1)S(1)} async-done(((bf16[8,128,512]{1,2,0:T(8,128)(2,1)}), bf16[8,128,512]{1,2,0:T(8,128)(2,1)S(1)}, u32[]{:S(2)}, u32[]{:S(2)}) %all-to-all-start.2) | async-done | bytes 1048608 | tf_op jit(solution)/shard_map/all_to_all | solution.py:57
  313.3 0.6 multiply_reduce_fusion
  313.8 4.7 %convolution_bitcast_fusion = f32[128,1,6,128]{0,3,2,1:T(8,128)S(1)} fusion(bf16[6,128,4096]{2,1,0:T(8,128)(2,1)} %bitcast.94, f32[128,4096]{1,0:T(8,128)S(1)} %get-tuple-element.31, f32[4096]{0:T(1024)S(1)} %copy-done.3, f32[128]{0:T(128)S(1)} %add_rsqrt_fusion.1), kind=kOutput, calls=%fused_computation.31 | convolution fusion | flops 806879232 | bytes 8798720 | tf_op jit(solution)/shard_map/dot_general | solution.py:212
  318.6 1.2 fusion.13
  (63 shorter events, 3.1 us)
Async XLA Ops:
  6.5 16.8 %copy-start.1 = (bf16[512,64]{0,1:T(8,128)(2,1)S(1)}, bf16[512,64]{0,1:T(8,128)(2,1)}, u32[]{:S(2)}) copy-start(bf16[512,64]{0,1:T(8,128)(2,1)} %param.13) | copy-start | bytes 196612
  6.5 16.9 %collective-permute-start.4 = (bf16[512,64]{0,1:T(8,128)(2,1)}, bf16[512,64]{0,1:T(8,128)(2,1)S(1)}, u32[]{:S(2)}, u32[]{:S(2)}) collective-permute-start(bf16[512,64]{0,1:T(8,128)(2,1)} %param.13), channel_id=1, source_target_pairs={{0,112},{16,0},{32,16},{48,32},{64,48},{80,64},{96,80},{112,96},{1... | collective-permute-start | bytes 196616 | tf_op jit(solution)/shard_map/ppermute | solution.py:63
  12.6 10.8 %collective-permute-start.5 = (bf16[512,64]{0,1:T(8,128)(2,1)}, bf16[512,64]{0,1:T(8,128)(2,1)S(1)}, u32[]{:S(2)}, u32[]{:S(2)}) collective-permute-start(bf16[512,64]{0,1:T(8,128)(2,1)} %param.13), channel_id=1, source_target_pairs={{0,16},{16,32},{32,48},{48,64},{64,80},{80,96},{96,112},{112,0},{1... | collective-permute-start | bytes 196616 | tf_op jit(solution)/shard_map/ppermute | solution.py:63
  16.5 14.0 %collective-permute-start = (bf16[128,512]{1,0:T(8,128)(2,1)S(1)}, bf16[128,512]{1,0:T(8,128)(2,1)S(1)}, u32[]{:S(2)}, u32[]{:S(2)}) collective-permute-start(bf16[128,512]{1,0:T(8,128)(2,1)S(1)} %multiply_convert_fusion.1), channel_id=1, source_target_pairs={{0,8},{8,0},{1,9},{9,1},{2,10},{10,2},{3,11},{11,3},{4,12},{12,4},... | collective-permute-start | bytes 393224 | tf_op jit(solution)/shard_map/ppermute | solution.py:121
  23.4 15.6 %collective-permute-start.6 = (bf16[3,512,64]{1,2,0:T(8,128)(2,1)S(1)}, bf16[3,512,64]{1,2,0:T(8,128)(2,1)S(1)}, u32[]{:S(2)}, u32[]{:S(2)}) collective-permute-start(bf16[3,512,64]{1,2,0:T(8,128)(2,1)S(1)} %pad_maximum_fusion.3), channel_id=1, source_target_pairs={{0,80},{16,96},{32,112},{48,0},{64,16},{80,32},{96,48},{112,64},{1... | collective-permute-start | bytes 589832 | tf_op jit(solution)/shard_map/ppermute | solution.py:63
  25.4 19.7 %collective-permute-start.7 = (bf16[3,512,64]{1,2,0:T(8,128)(2,1)S(1)}, bf16[3,512,64]{1,2,0:T(8,128)(2,1)S(1)}, u32[]{:S(2)}, u32[]{:S(2)}) collective-permute-start(bf16[3,512,64]{1,2,0:T(8,128)(2,1)S(1)} %pad_maximum_fusion.3), channel_id=1, source_target_pairs={{0,48},{16,64},{32,80},{48,96},{64,112},{80,0},{96,16},{112,32},{1... | collective-permute-start | bytes 589832 | tf_op jit(solution)/shard_map/ppermute | solution.py:63
  30.6 16.0 %collective-permute-start.3 = (bf16[2,128,512]{2,1,0:T(8,128)(2,1)S(1)}, bf16[2,128,512]{2,1,0:T(8,128)(2,1)S(1)}, u32[]{:S(2)}, u32[]{:S(2)}) collective-permute-start(bf16[2,128,512]{2,1,0:T(8,128)(2,1)S(1)} %get-tuple-element.24), channel_id=1, source_target_pairs={{0,128},{128,256},{256,384},{384,0},{1,129},{129,257},{257,385},{3... | collective-permute-start | bytes 786440 | tf_op jit(solution)/shard_map/ppermute | solution.py:63
  32.5 14.1 %collective-permute-start.2 = (bf16[2,128,512]{2,1,0:T(8,128)(2,1)S(1)}, bf16[2,128,512]{2,1,0:T(8,128)(2,1)S(1)}, u32[]{:S(2)}, u32[]{:S(2)}) collective-permute-start(bf16[2,128,512]{2,1,0:T(8,128)(2,1)S(1)} %get-tuple-element.24), channel_id=1, source_target_pairs={{0,256},{128,384},{256,0},{384,128},{1,257},{129,385},{257,1},{385... | collective-permute-start | bytes 786440 | tf_op jit(solution)/shard_map/ppermute | solution.py:63
  34.5 14.6 %collective-permute-start.1 = (bf16[2,128,512]{2,1,0:T(8,128)(2,1)S(1)}, bf16[2,128,512]{2,1,0:T(8,128)(2,1)S(1)}, u32[]{:S(2)}, u32[]{:S(2)}) collective-permute-start(bf16[2,128,512]{2,1,0:T(8,128)(2,1)S(1)} %get-tuple-element.24), channel_id=1, source_target_pairs={{0,384},{128,0},{256,128},{384,256},{1,385},{129,1},{257,129},{385... | collective-permute-start | bytes 786440 | tf_op jit(solution)/shard_map/ppermute | solution.py:63
  49.9 5.0 %collective-permute-start.8 = (bf16[4,128,8,64]{1,3,2,0:T(8,128)(2,1)S(1)}, bf16[4,128,8,64]{1,3,2,0:T(8,128)(2,1)S(1)}, u32[]{:S(2)}, u32[]{:S(2)}) collective-permute-start(bf16[4,128,8,64]{1,3,2,0:T(8,128)(2,1)S(1)} %get-tuple-element.20), channel_id=1, source_target_pairs={{0,8},{8,0},{1,9},{9,1},{2,10},{10,2},{3,11},{11,3},{4,12},{12,4},... | collective-permute-start | bytes 1572872 | tf_op jit(solution)/shard_map/ppermute | solution.py:131
  54.9 10.6 %collective-permute-start.11 = (bf16[128,8,2,64]{0,3,1,2:T(8,128)(2,1)S(1)}, bf16[128,8,2,64]{0,3,1,2:T(8,128)(2,1)S(1)}, u32[]{:S(2)}, u32[]{:S(2)}) collective-permute-start(bf16[128,8,2,64]{0,3,1,2:T(8,128)(2,1)S(1)} %get-tuple-element.17), channel_id=1, source_target_pairs={{0,128},{128,256},{256,384},{384,0},{1,129},{129,257},{257,385},{3... | collective-permute-start | bytes 786440 | tf_op jit(solution)/shard_map/ppermute | solution.py:63
  56.9 15.2 %collective-permute-start.10 = (bf16[128,8,2,64]{0,3,1,2:T(8,128)(2,1)S(1)}, bf16[128,8,2,64]{0,3,1,2:T(8,128)(2,1)S(1)}, u32[]{:S(2)}, u32[]{:S(2)}) collective-permute-start(bf16[128,8,2,64]{0,3,1,2:T(8,128)(2,1)S(1)} %get-tuple-element.18), channel_id=1, source_target_pairs={{0,256},{128,384},{256,0},{384,128},{1,257},{129,385},{257,1},{385... | collective-permute-start | bytes 786440 | tf_op jit(solution)/shard_map/ppermute | solution.py:63
  62.3 11.1 %collective-permute-start.9 = (bf16[128,8,2,64]{0,3,1,2:T(8,128)(2,1)S(1)}, bf16[128,8,2,64]{0,3,1,2:T(8,128)(2,1)S(1)}, u32[]{:S(2)}, u32[]{:S(2)}) collective-permute-start(bf16[128,8,2,64]{0,3,1,2:T(8,128)(2,1)S(1)} %get-tuple-element.16), channel_id=1, source_target_pairs={{0,384},{128,0},{256,128},{384,256},{1,385},{129,1},{257,129},{385... | collective-permute-start | bytes 786440 | tf_op jit(solution)/shard_map/ppermute | solution.py:63
  74.6 7.4 %copy-start = (bf16[512,512]{1,0:T(8,128)(2,1)S(1)}, bf16[512,512]{1,0:T(8,128)(2,1)}, u32[]{:S(2)}) copy-start(bf16[512,512]{1,0:T(8,128)(2,1)} %param.12) | copy-start | bytes 1572868
  75.7 7.3 %copy-start.5 = (s32[128,2]{0,1:T(2,128)S(1)}, s32[128,2]{0,1:T(2,128)}, u32[]{:S(2)}) copy-start(s32[128,2]{0,1:T(2,128)} %param.18) | copy-start | bytes 3076
  75.7 7.3 %copy-start.6 = (s32[128]{0:T(128)S(1)}, s32[128]{0:T(128)}, u32[]{:S(2)}) copy-start(s32[128]{0:T(128)} %param.19) | copy-start | bytes 1540
  75.7 35.5 %all-to-all-start = ((bf16[8,128,512]{1,2,0:T(8,128)(2,1)}), bf16[8,128,512]{1,2,0:T(8,128)(2,1)S(1)}, u32[]{:S(2)}, u32[]{:S(2)}) async-start(bf16[8,128,512]{1,2,0:T(8,128)(2,1)} %bitcast.27), calls=%async_computation | async-start | bytes 2097152 | tf_op jit(solution)/shard_map/all_to_all | solution.py:149
  82.0 29.5 %copy-start.4 = (f32[512]{0:T(512)S(1)}, f32[512]{0:T(512)}, u32[]{:S(2)}) copy-start(f32[512]{0:T(512)} %param.14) | copy-start | bytes 6148
  82.3 49.5 %copy-start.2 = (bf16[64,768]{1,0:T(8,128)(2,1)S(1)}, bf16[64,768]{1,0:T(8,128)(2,1)}, u32[]{:S(2)}) copy-start(bf16[64,768]{1,0:T(8,128)(2,1)} %param.21) | copy-start | bytes 294916
  135.3 146.4 %all-to-all-start.3 = ((bf16[64,64,768]{2,1,0:T(8,128)(2,1)}), bf16[64,64,768]{2,1,0:T(8,128)(2,1)}, u32[]{:S(2)}, u32[]{:S(2)}) async-start(bf16[64,64,768]{2,1,0:T(8,128)(2,1)} %stack.57), calls=%async_computation.3 | async-start | bytes 12582912 | tf_op jit(solution)/shard_map/all_to_all | solution.py:194
  140.8 145.8 %all-gather.3.cloned.1.call-start = ((), (), s32[]{:S(2)}) async-start(), calls=%async_computation.4 | async-start | bytes 2359296 | tf_op jit(solution)/shard_map/all_gather | solution.py:192
  282.8 30.2 %all-to-all-start.2 = ((bf16[8,128,512]{1,2,0:T(8,128)(2,1)}), bf16[8,128,512]{1,2,0:T(8,128)(2,1)S(1)}, u32[]{:S(2)}, u32[]{:S(2)}) async-start(bf16[8,128,512]{1,2,0:T(8,128)(2,1)} %broadcast_in_dim.28), calls=%async_computation.2 | async-start | bytes 2097152 | tf_op jit(solution)/shard_map/all_to_all | solution.py:57
  290.9 8.6 %copy-start.3 = (f32[4096]{0:T(1024)S(1)}, f32[4096]{0:T(1024)}, u32[]{:S(2)}) copy-start(f32[4096]{0:T(1024)} %param.20) | copy-start | bytes 49156
Sparse Core Ops, SparseCore 0:
  143.7 36.4 all-gather.2
